TPU v7x, 128 devices: a whole 4x4x4 slice. The times are simulated.
128 devices in a mesh: req: 16 (over y, z), mlp: 8 (over x, core).
Axes of the slice: x: 4, y: 4, z: 4, core: 2. Of those that a mesh axis runs over, the one named last changes fastest.
Arguments:
- tokens: bfloat16 [32768, 1536], P(('req', 'mlp')), may hold values from -6 to 6
- attn_gain: float32 [1536], replicated, may hold values from 0.1 to 1.9
- w_query: bfloat16 [1536, 1536], replicated, may hold values from -0.15625 to 0.15625
- w_keyval: bfloat16 [1536, 256], replicated, may hold values from -0.15625 to 0.15625
- w_out: bfloat16 [1536, 1536], replicated, may hold values from -0.15625 to 0.15625
- ffn_gain: float32 [1536], replicated, may hold values from 0.1 to 1.9
- w_gate: bfloat16 [1536, 4608], P('req', 'mlp'), may hold values from -0.15625 to 0.15625
- w_up: bfloat16 [1536, 4608], P('req', 'mlp'), may hold values from -0.15625 to 0.15625
- w_down: bfloat16 [1536, 4608], P('req', 'mlp'), may hold values from -0.09375 to 0.09375
- prefix_kv: bfloat16 [2, 128, 512, 256], P(None, 'req'), may hold values from -60 to 60, as said below
- own_prefix: bfloat16 [16, 512, 256], P('req'), may hold values from -60 to 60, as said below
- leaf_parent: int32 [16], replicated, may hold values from 0 to 127
- node_parent: int32 [128], replicated, may hold values from 0 to 127
- seg_lengths: int32 [3, 128], replicated, may hold values from 1 to 512
Outputs:
- layer_out: bfloat16 [32768, 1536], P(('req', 'mlp'))
Inputs may be any that keep to these rules, and one draw needn't show every extreme that they name: `prefix_kv`: columns below 128 are keys, the rest values. `own_prefix`: columns below 128 are keys, the rest values.
All inputs are finite; a program needn't handle non-finite values.
Results may differ from a plain program's by a relative error of at most 0.018.
Values may be sent and summed in bfloat16 or wider, within the bound.
No kernel may reach another device: no remote copies, remote signals or barrier semaphores. Data moves between devices by JAX's collectives and lax.ppermute only.
A program may use at most 192 MiB of HBM per device.

v0:
```python
import jax
import jax.numpy as jnp
from jax import lax
from jax.sharding import PartitionSpec as P

HEADS = 12
HD = 128
WINDOW = 1024
EPS = 1e-06


def rms_scale(values, gain):
    wide = values.astype(jnp.float32)
    return wide * lax.rsqrt(jnp.mean(wide * wide, axis=-1, keepdims=True) + EPS) * gain


def rotate(values, where_at):
    half_dim = values.shape[-1] // 2
    freqs = 10000.0 ** (-jnp.arange(half_dim, dtype=jnp.float32) / half_dim)
    angles = where_at.astype(jnp.float32)[:, None] * freqs[None, :]
    cosine = jnp.cos(angles)[:, None, :]
    sine = jnp.sin(angles)[:, None, :]
    first = values[..., :half_dim]
    second = values[..., half_dim:]
    return jnp.concatenate([first * cosine - second * sine, first * sine + second * cosine], -1)


def body(
    tokens,
    attn_gain,
    w_query,
    w_keyval,
    w_out,
    ffn_gain,
    w_gate,
    w_up,
    w_down,
    prefix_kv,
    own_prefix,
    leaf_parent,
    node_parent,
    seg_lengths,
):
    tok_rows = tokens.shape[0]
    mine = lax.axis_index("req")
    n_mlp = lax.axis_size("mlp")
    position_group = lax.axis_index("mlp")
    node_dev = prefix_kv.shape[1]
    seg_slot = prefix_kv.shape[2]
    share = seg_slot // n_mlp
    leaf = leaf_parent[mine]
    upper = node_parent[leaf]
    len_zero = seg_lengths[0, upper]
    len_one = seg_lengths[1, leaf]
    len_two = seg_lengths[2, mine]
    total = len_zero + len_one + len_two
    ff_cols = w_gate.shape[1]
    packed = lax.all_gather(jnp.concatenate([w_gate, w_up, w_down], 1), "req", axis=0, tiled=True)
    down_full = packed[:, 2 * ff_cols :]
    level_zero = node_parent[leaf_parent]
    wanted = jnp.stack([level_zero, leaf_parent], 1)
    local_slot = wanted % node_dev
    my_rows = lax.dynamic_slice_in_dim(prefix_kv, position_group * share, share, 2)
    outgoing = my_rows[jnp.arange(2)[None, :], local_slot]
    arrived = lax.all_to_all(outgoing, "req", split_axis=0, concat_axis=0, tiled=True)
    owners = wanted[mine] // node_dev
    my_part = arrived[owners, jnp.arange(2)]
    levels = lax.all_gather(my_part, "mlp", axis=1, tiled=True)
    query_at = total + position_group * tok_rows + jnp.arange(tok_rows, dtype=jnp.int32)
    normed = rms_scale(tokens, attn_gain).astype(jnp.bfloat16)
    query_full = jnp.dot(normed, w_query, preferred_element_type=jnp.float32).reshape(
        tok_rows, HEADS, HD
    )
    queries = (rotate(query_full, query_at) * HD ** (-0.5)).astype(jnp.bfloat16)
    keyval_full = jnp.dot(normed, w_keyval, preferred_element_type=jnp.float32)
    new_keys = rotate(keyval_full[:, None, :HD], query_at)[:, 0].astype(jnp.bfloat16)
    new_vals = keyval_full[:, HD:].astype(jnp.bfloat16)
    new_keyval = jnp.concatenate([new_keys, new_vals], 1)
    piece = lax.all_gather(new_keyval, "mlp", axis=0, tiled=True)
    sources = jnp.concatenate([levels[0], levels[1], own_prefix[0], piece], 0)
    seq_len = 3 * seg_slot + piece.shape[0]
    span = WINDOW + tok_rows
    first = jnp.clip(total + position_group * tok_rows - WINDOW, 0, seq_len - span)
    key_at = first + jnp.arange(span, dtype=jnp.int32)
    len_cut = len_zero + len_one
    source_row = jnp.where(
        key_at < len_zero,
        key_at,
        jnp.where(
            key_at < len_cut,
            key_at - len_zero + seg_slot,
            jnp.where(
                key_at < total, key_at - len_cut + 2 * seg_slot, key_at - total + 3 * seg_slot
            ),
        ),
    )
    window = jnp.take(sources, source_row, axis=0, mode="clip")
    spacing = query_at[:, None] - key_at[None, :]
    allowed = ((spacing >= 0) & (spacing < WINDOW))[:, None, :]
    scores = jnp.einsum("thd,kd->thk", queries, window[:, :HD], preferred_element_type=jnp.float32)
    top = jnp.max(jnp.where(allowed, scores, -jnp.inf), axis=-1, keepdims=True)
    weights = jnp.where(allowed, jnp.exp(scores - top), 0.0)
    denom = jnp.sum(weights, axis=-1)
    mixed = jnp.einsum(
        "thk,kd->thd",
        weights.astype(jnp.bfloat16),
        window[:, HD:],
        preferred_element_type=jnp.float32,
    )
    context = (mixed / denom[..., None]).reshape(tok_rows, HEADS * HD).astype(jnp.bfloat16)
    attn_out = jnp.dot(context, w_out, preferred_element_type=jnp.float32)
    resid = (tokens.astype(jnp.float32) + attn_out).astype(jnp.bfloat16)
    ffn_in = rms_scale(resid, ffn_gain).astype(jnp.bfloat16)
    all_rows = lax.all_gather(ffn_in, "mlp", axis=0, tiled=True)
    gate_up = jnp.dot(all_rows, packed[:, : 2 * ff_cols], preferred_element_type=jnp.float32)
    gate = gate_up[:, :ff_cols]
    upward = gate_up[:, ff_cols:]
    hidden = (jax.nn.gelu(gate, approximate=True) * upward).astype(jnp.bfloat16)
    summed = lax.psum_scatter(
        lax.dot_general(
            hidden, down_full, (((1,), (1,)), ((), ())), preferred_element_type=jnp.float32
        ).astype(jnp.bfloat16),
        "mlp",
        scatter_dimension=0,
        tiled=True,
    ).astype(jnp.float32)
    return (resid.astype(jnp.float32) + summed).astype(jnp.bfloat16)


def solution(mesh):
    return jax.shard_map(
        body,
        mesh=mesh,
        in_specs=(
            P(("req", "mlp"), None),
            P(),
            P(),
            P(),
            P(),
            P(),
            P("req", "mlp"),
            P("req", "mlp"),
            P("req", "mlp"),
            P(None, "req", None, None),
            P("req", None, None),
            P(),
            P(),
            P(),
        ),
        out_specs=P(("req", "mlp"), None),
        check_vma=False,
    )
```

profile of v0, /device:TPU:1, one launch (start us, length us, event | category | flops | bytes accessed | tf_op | source)
XLA Modules:
  0.0 221.3 jit_solution(13196897716380005611)
XLA Ops:
  6.5 0.0 copy-start
  6.5 1.3 dynamic_slice.21
  9.8 1.2 dynamic_slice.22
  12.4 1.4 fusion.29
  13.7 0.0 copy-start.6
  13.7 0.0 copy-start.7
  13.8 0.0 copy-start.10
  13.8 0.0 copy-start.2
  13.8 1.8 fusion.37
  16.3 0.7 constant_dynamic-slice_fusion.2
  18.9 0.3 fusion.46
  19.3 0.7 pad_maximum_fusion.1
  19.9 0.0 all-gather.4.cloned.1.call-update
  19.9 0.0 all-gather.8.cloned.1.call-start
  20.0 0.9 concatenate.47
  20.9 0.0 all-gather.8.cloned.1.call-update
  21.0 0.7 gather_fusion
  21.7 0.1 copy.32
  21.7 0.1 reshape.414
  21.8 1.1 constant_dynamic-slice_fusion
  22.9 0.0 copy-start.3
  22.9 0.0 copy-start.13
  22.9 1.6 gather_fusion.1
  24.5 8.6 %all-to-all-start = ((bf16[16,2,64,256]{3,2,1,0:T(8,128)(2,1)}), bf16[16,2,64,256]{3,2,1,0:T(8,128)(2,1)}, u32[]{:S(2)}, u32[]{:S(2)}) async-start(bf16[16,2,64,256]{3,2,1,0:T(8,128)(2,1)} %bitcast.8), calls=%async_computation | async-start | bytes 2097152 | tf_op jit(solution)/shard_map/all_to_all | solution.py:65
  33.2 0.0 all-gather.6.cloned.1.call-start
  33.3 0.2 dynamic-slice_reduce_fusion
  33.5 0.5 fusion.57
  34.0 1.2 multiply_cosine_fusion
  35.2 4.4 %fusion.39 = f32[256,1536]{0,1:T(8,128)S(1)} fusion(bf16[1536,1536]{1,0:T(8,128)(2,1)} %param.16, bf16[256,1536]{1,0:T(8,128)(2,1)S(1)} %copy-done.3, f32[1536]{0:T(1024)S(1)} %copy-done.13, f32[256]{0:T(256)S(1)} %add_rsqrt_fusion.1), kind=kOutput, calls=%fused_computation.55 | convolution fusion | flops 1209532416 | bytes 7085056 | tf_op jit(solution)/shard_map/dot_general | solution.py:71
  39.6 0.0 copy-start.4
  39.6 1.0 fusion.64
  40.6 0.6 iota_add_fusion.1
  41.2 0.1 copy.36
  41.3 1.6 copy.40
  43.0 1.7 copy.41
  44.6 0.7 fusion.49
  45.3 3.5 %multiply_subtract_fusion = (f32[256,12,64]{2,0,1:T(8,128)}, f32[256,12,64]{2,0,1:T(8,128)}) fusion(f32[256,12,64]{2,0,1:T(8,128)} %copy.41, f32[256,12,64]{2,0,1:T(8,128)S(1)} %copy.40, f32[256,64]{1,0:T(8,128)} %get-tuple-element.17, f32[256,64]{1,0:T(8,128)S(1)} %get-tuple-element.16), kind=kLoop, calls=%fused_computation.49 | loop fusion | flops 1179648 | bytes 3276800 | tf_op jit(solution)/shard_map/sub | solution.py:25
  48.8 1.1 fusion.35
  49.9 0.0 all-to-all-done
  49.9 1.8 gather_fusion.2
  51.7 0.1 copy.33
  51.8 15.5 %all_gather.12 = bf16[2,512,256]{2,0,1:T(2,128)(2,1)S(1)} all-gather(bf16[2,64,256]{2,0,1:T(2,128)(2,1)S(1)} %copy.33), channel_id=1, replica_groups=mesh['req'=16,'mlp'=8] {'mlp'}, dimensions={1}, use_global_device_ids=true | all-gather | bytes 589824 | tf_op jit(solution)/shard_map/all_gather | solution.py:68
  67.2 0.7 fusion.65
  68.0 0.7 copy.42
  68.7 0.7 copy.43
  69.3 0.0 all-gather.4.cloned.1.call-done
  69.4 2.6 %pad_maximum_fusion = bf16[3584,256]{0,1:T(8,128)(2,1)} fusion(bf16[2048,256]{0,1:T(8,128)(2,1)} %all-gather.4.cloned.1.call-done, bf16[512,256]{0,1:T(8,128)(2,1)S(1)} %bitcast.59, bf16[512,256]{0,1:T(8,128)(2,1)S(1)} %bitcast.58, bf16[512,256]{0,1:T(8,128)(2,1)S(1)} %bitcast.57), kind=kLoop, calls=%fused_computation.38 | loop fusion | flops 7340032 | bytes 3670016 | tf_op jit(solution)/shard_map/concatenate | solution.py:80
  72.0 2.9 %copy.37 = bf16[3584,256]{1,0:T(8,128)(2,1)S(1)} copy(bf16[3584,256]{0,1:T(8,128)(2,1)} %pad_maximum_fusion) | data formatting | bytes 3670016 | tf_op jit(solution)/shard_map/concatenate | solution.py:80
  74.9 4.1 %gather_fusion.3 = bf16[1280,256]{1,0:T(8,128)(2,1)S(1)} fusion(bf16[3584,256]{1,0:T(8,128)(2,1)S(1)} %copy.37, s32[2048]{0:T(1024)S(1)} %pad_clamp_fusion), kind=kCustom, calls=%fused_computation.3 | custom fusion | bytes 1315840 | tf_op jit(solution)/shard_map/jit(_take)/gather | solution.py:97
  79.0 11.3 %fusion.66 = (f32[256,12]{0,1:T(8,128)S(1)}, bf16[256,12,1280]{2,0,1:T(8,128)(2,1)}) fusion(pred[256,1280]{1,0:T(8,128)(4,1)} %fusion.35, bf16[1280,256]{1,0:T(8,128)(2,1)S(1)} %gather_fusion.3, f32[256,12,64]{2,0,1:T(8,128)} %get-tuple-element.6, f32[256,12,64]{2,0,1:T(8,128)} %get-tuple-element.5), kind=kOutput, calls=%fused_computation.116 | convolution fusion | flops 2035287296 | bytes 15478784 | tf_op jit(solution)/shard_map/sub | solution.py:102
  90.3 6.0 %divide_convert_fusion = bf16[256,12,128]{0,2,1:T(8,128)(2,1)S(1)} fusion(bf16[256,12,1280]{2,0,1:T(8,128)(2,1)} %get-tuple-element.19, f32[256,12]{0,1:T(8,128)S(1)} %get-tuple-element.18, bf16[1280,256]{1,0:T(8,128)(2,1)S(1)} %gather_fusion.3), kind=kOutput, calls=%fused_computation.47 | convolution fusion | flops 1007419392 | bytes 8994816 | tf_op jit(solution)/shard_map/thk,kd->thd/dot_general | solution.py:104
  96.4 0.0 copy-start.8
  96.4 3.9 %multiply_reduce_fusion = (f32[256]{0:T(256)S(1)}, f32[256,1536]{1,0:T(8,128)S(1)}) fusion(bf16[256,1536]{0,1:T(8,128)(2,1)S(1)} %bitcast.55, bf16[1536,1536]{1,0:T(8,128)(2,1)} %param.18, bf16[256,1536]{1,0:T(8,128)(2,1)S(1)} %copy-done.3), kind=kOutput, calls=%fused_computation.46 | convolution fusion | flops 1210318592 | bytes 7865344 | tf_op jit(solution)/shard_map/dot_general | solution.py:111
  100.3 1.1 multiply_convert_fusion
  101.4 0.0 all-gather.6.cloned.1.call-update
  101.4 0.3 reduce-scatter.2.cloned.1.call-start
  101.7 5.8 %all-gather.8.cloned.1.call-done = bf16[1536,1728]{1,0:T(8,128)(2,1)} async-done(((bf16[96,1728]{1,0:T(8,128)(2,1)}), bf16[1536,1728]{1,0:T(8,128)(2,1)}) %all-gather.8.cloned.1.call-update) | async-done | bytes 5308432 | tf_op jit(solution)/shard_map/all_gather | solution.py:58
  107.5 42.6 %all-gather.6.cloned.1.call-done = bf16[2048,1536]{1,0:T(8,128)(2,1)} async-done(((bf16[256,1536]{1,0:T(8,128)(2,1)}), bf16[2048,1536]{1,0:T(8,128)(2,1)}) %all-gather.6.cloned.1.call-update) | async-done | bytes 6291472 | tf_op jit(solution)/shard_map/all_gather | solution.py:114
  150.1 11.1 %fusion.17 = f32[2048,1152]{0,1:T(8,128)S(1)} fusion(bf16[2048,1536]{1,0:T(8,128)(2,1)} %all-gather.6.cloned.1.call-done, bf16[1536,1728]{1,0:T(8,128)(2,1)} %all-gather.8.cloned.1.call-done), kind=kOutput, calls=%fused_computation.23 | convolution fusion | flops 7247757312 | bytes 19267584 | tf_op jit(solution)/shard_map/dot_general | solution.py:115
  161.2 9.6 %convolution_convert_fusion = bf16[2048,1536]{1,0:T(8,128)(2,1)} fusion(f32[2048,1152]{0,1:T(8,128)S(1)} %fusion.17, bf16[1536,1728]{1,0:T(8,128)(2,1)} %all-gather.8.cloned.1.call-done), kind=kOutput, calls=%fused_computation.12 | convolution fusion | flops 3638820864 | bytes 17694720 | tf_op jit(solution)/shard_map/dot_general | solution.py:120
  170.8 0.0 reduce-scatter.2.cloned.1.call-update
  170.8 0.0 copy-start.1
  170.8 41.7 %reduce-scatter.2.cloned.1.call-done = bf16[256,1536]{1,0:T(8,128)(2,1)} async-done(((bf16[2048,1536]{1,0:T(8,128)(2,1)}), bf16[256,1536]{1,0:T(8,128)(2,1)}) %reduce-scatter.2.cloned.1.call-update) | async-done | bytes 786448 | tf_op jit(solution)/shard_map/reduce_scatter | solution.py:119
  212.5 2.2 add_convert_fusion
  (32 shorter events, 0.1 us)
Async XLA Ops:
  6.5 7.2 %copy-start = (bf16[1536,256]{1,0:T(8,128)(2,1)S(1)}, bf16[1536,256]{1,0:T(8,128)(2,1)}, u32[]{:S(2)}) copy-start(bf16[1536,256]{1,0:T(8,128)(2,1)} %param.17) | copy-start | bytes 2359300
  6.5 9.8 %copy-start.11 = (s32[3,128]{1,0:T(4,128)S(1)}, s32[3,128]{1,0:T(4,128)}, u32[]{:S(2)}) copy-start(s32[3,128]{1,0:T(4,128)} %param.27) | copy-start | bytes 4612
  6.5 62.8 %all-gather.4.cloned.1.call-start = ((), (), s32[]{:S(2)}) async-start(), calls=%async_computation.2 | async-start | bytes 1179648 | tf_op jit(solution)/shard_map/all_gather | solution.py:79
  13.7 6.3 %copy-start.5 = (bf16[96,576]{1,0:T(8,128)(2,1)S(1)}, bf16[96,576]{1,0:T(8,128)(2,1)}, u32[]{:S(2)}) copy-start(bf16[96,576]{1,0:T(8,128)(2,1)} %param.20) | copy-start | bytes 331780
  13.7 6.3 %copy-start.6 = (bf16[96,576]{1,0:T(8,128)(2,1)S(1)}, bf16[96,576]{1,0:T(8,128)(2,1)}, u32[]{:S(2)}) copy-start(bf16[96,576]{1,0:T(8,128)(2,1)} %param.21) | copy-start | bytes 331780
  13.7 6.3 %copy-start.7 = (bf16[96,576]{1,0:T(8,128)(2,1)S(1)}, bf16[96,576]{1,0:T(8,128)(2,1)}, u32[]{:S(2)}) copy-start(bf16[96,576]{1,0:T(8,128)(2,1)} %param.22) | copy-start | bytes 331780
  13.8 7.1 %copy-start.10 = (s32[16]{0:T(128)S(1)}, s32[16]{0:T(128)}, u32[]{:S(2)}) copy-start(s32[16]{0:T(128)} %param.25) | copy-start | bytes 196
  13.8 7.2 %copy-start.2 = (s32[128]{0:T(128)S(1)}, s32[128]{0:T(128)}, u32[]{:S(2)}) copy-start(s32[128]{0:T(128)} %param.26) | copy-start | bytes 1540
  19.9 87.6 %all-gather.8.cloned.1.call-start = ((), (), s32[]{:S(2)}) async-start(), calls=%async_computation.4 | async-start | bytes 5849088 | tf_op jit(solution)/shard_map/all_gather | solution.py:58
  22.9 12.3 %copy-start.3 = (bf16[256,1536]{1,0:T(8,128)(2,1)S(1)}, bf16[256,1536]{1,0:T(8,128)(2,1)}, u32[]{:S(2)}) copy-start(bf16[256,1536]{1,0:T(8,128)(2,1)} %param.14) | copy-start | bytes 2359300
  22.9 12.3 %copy-start.13 = (f32[1536]{0:T(1024)S(1)}, f32[1536]{0:T(1024)}, u32[]{:S(2)}) copy-start(f32[1536]{0:T(1024)} %param.15) | copy-start | bytes 18436
  24.5 25.4 %all-to-all-start = ((bf16[16,2,64,256]{3,2,1,0:T(8,128)(2,1)}), bf16[16,2,64,256]{3,2,1,0:T(8,128)(2,1)}, u32[]{:S(2)}, u32[]{:S(2)}) async-start(bf16[16,2,64,256]{3,2,1,0:T(8,128)(2,1)} %bitcast.8), calls=%async_computation | async-start | bytes 2097152 | tf_op jit(solution)/shard_map/all_to_all | solution.py:65
  33.2 116.9 %all-gather.6.cloned.1.call-start = ((), (), s32[]{:S(2)}) async-start(), calls=%async_computation.3 | async-start | bytes 7077888 | tf_op jit(solution)/shard_map/all_gather | solution.py:114
  39.6 1.6 copy-start.4
  45.3 3.5 %copy-start.12 = (s32[256]{0:T(256)S(1)}, s32[256]{0:T(256)}, u32[]{:S(2)}) copy-start(s32[256]{0:T(256)} %iota_add_fusion.1) | copy-start | bytes 3076
  45.3 4.6 %copy-start.9 = (s32[2]{0:T(128)S(1)}, s32[2]{0:T(128)}, u32[]{:S(2)}) copy-start(s32[2]{0:T(128)} %fusion.57) | copy-start | bytes 28
  96.4 4.0 %copy-start.8 = (f32[1536]{0:T(1024)S(1)}, f32[1536]{0:T(1024)}, u32[]{:S(2)}) copy-start(f32[1536]{0:T(1024)} %param.19) | copy-start | bytes 18436
  101.4 111.1 %reduce-scatter.2.cloned.1.call-start = ((), (), s32[]{:S(2)}) async-start(), calls=%async_computation.5 | async-start | bytes 7077888 | tf_op jit(solution)/shard_map/reduce_scatter | solution.py:119
  170.8 43.9 %copy-start.1 = (bf16[1536,256]{1,0:T(8,128)(2,1)S(1)}, bf16[1536,256]{1,0:T(8,128)(2,1)}, u32[]{:S(2)}) copy-start(bf16[1536,256]{1,0:T(8,128)(2,1)} %param.17) | copy-start | bytes 2359300
Sparse Core Ops, SparseCore 0:
  20.1 26.9 all-gather.3
  49.2 58.2 all-gather.7
  109.2 40.8 all-gather.5
  170.9 41.5 reduce-scatter.1
where the time goes:
time: 222 us; the launch traced here: 221 us
  waiting for transfers between devices  90.2 us (41%)
  matrix products  48.2 us (22%)
  local copies, waits for them, and re-layouts  23.2 us (10%)
  between operations  19.3 us (9%)
  other arithmetic  15.9 us (7%)
  blocking collectives  15.5 us (7%)
  starting transfers between devices  9 us (4%)
    all_gather x1, waiting for transfers between devices, body(): all_rows = lax.all_gather(ffn_in, 'mlp', axis=0, tiled=True)  42.6 us
    reduce_scatter x1, waiting for transfers between devices, body(): lax.psum_scatter(lax.dot_general(hidden, down_full, (((1,), (1,)), ((), (...  41.7 us
    all_gather x1, blocking collectives, body(): levels = lax.all_gather(my_part, 'mlp', axis=1, tiled=True)  15.5 us
    sub x1, matrix products, body(): weights = jnp.where(allowed, jnp.exp(scores - top), 0.0)  11.3 us
    dot_general x1, matrix products, body(): jnp.dot(all_rows, packed[:, :2 * ff_cols], preferred_element_type=jnp.flo...  11.1 us
    dot_general x1, matrix products, body(): lax.dot_general(hidden, down_full, (((1,), (1,)), ((), ())), preferred_el...  9.57 us
    all_to_all x1, starting transfers between devices, body(): lax.all_to_all(outgoing, 'req', split_axis=0, concat_axis=0, tiled=True)  8.65 us
    dot_general x1, matrix products, body(): jnp.einsum('thk,kd->thd', weights.astype(jnp.bfloat16), window[:, HD:], p...  6.03 us
  transfers between devices with their start and end apart: 5, of which 3 were waited for; matrix products, arithmetic and copies ran while one was open for 26% of the time, Pallas kernels for 0%

commit v1 on v0

--- a/solution.py
+++ b/solution.py
@@ -55,7 +55,15 @@
     len_two = seg_lengths[2, mine]
     total = len_zero + len_one + len_two
     ff_cols = w_gate.shape[1]
-    packed = lax.all_gather(jnp.concatenate([w_gate, w_up, w_down], 1), "req", axis=0, tiled=True)
+    packed = jnp.concatenate(
+        lax.all_to_all(
+            jnp.stack([jnp.concatenate([w_gate, w_up, w_down], 1)] * lax.axis_size("req")),
+            "req",
+            0,
+            0,
+        ),
+        axis=0,
+    )
     down_full = packed[:, 2 * ff_cols :]
     level_zero = node_parent[leaf_parent]
     wanted = jnp.stack([level_zero, leaf_parent], 1)

time: 222 us -> 240 us (1.081)
  blocking collectives: 15.5 us -> 85.3 us
  waiting for transfers between devices: 90.2 us -> 40.3 us
    all_to_all x0 -> x1, blocking collectives: none -> 68.8 us  [body(): lax.all_to_all(jnp.stack([jnp.concatenate([w_gate, w_up, w_down], 1)] * l...]
    all_gather x1, waiting for transfers between devices: 42.6 us -> 0.01 us  [body(): all_rows = lax.all_gather(ffn_in, 'mlp', axis=0, tiled=True)]
    all_gather x1 -> x0, waiting for transfers between devices: 5.82 us -> none  [body(): lax.all_gather(jnp.concatenate([w_gate, w_up, w_down], 1), 'req', axis=0,...]
    unnamed x33 -> x31, local copies, waits for them, and re-layouts: 4.84 us -> 4.79 us
  transfers between devices with their start and end apart: 5 -> 4, of which waited for: 3 -> 1; matrix products, arithmetic and copies ran while one was open for 26% -> 10% of each run, Pallas kernels for 0% -> 0%
where the time goes in v1:
time: 240 us
  blocking collectives  85.3 us (36%)
  matrix products  48.1 us (20%)
  waiting for transfers between devices  40.3 us (17%)
  local copies, waits for them, and re-layouts  23 us (10%)
  between operations  19.3 us (8%)
  other arithmetic  14.9 us (6%)
  starting transfers between devices  8.73 us (4%)
    all_to_all x1, blocking collectives, body(): lax.all_to_all(jnp.stack([jnp.concatenate([w_gate, w_up, w_down], 1)] * l...  68.8 us
    reduce_scatter x1, waiting for transfers between devices, body(): lax.psum_scatter(lax.dot_general(hidden, down_full, (((1,), (1,)), ((), (...  40.2 us
    all_gather x1, blocking collectives, body(): levels = lax.all_gather(my_part, 'mlp', axis=1, tiled=True)  16.5 us
    sub x1, matrix products, body(): weights = jnp.where(allowed, jnp.exp(scores - top), 0.0)  11.6 us
    dot_general x1, matrix products, body(): jnp.dot(all_rows, packed[:, :2 * ff_cols], preferred_element_type=jnp.flo...  11.1 us
    dot_general x1, matrix products, body(): lax.dot_general(hidden, down_full, (((1,), (1,)), ((), ())), preferred_el...  9.57 us
    all_to_all x1, starting transfers between devices, body(): lax.all_to_all(outgoing, 'req', split_axis=0, concat_axis=0, tiled=True)  8.65 us
    dot_general x1, matrix products, body(): jnp.einsum('thk,kd->thd', weights.astype(jnp.bfloat16), window[:, HD:], p...  5.92 us
  transfers between devices with their start and end apart: 4, of which 1 were waited for; matrix products, arithmetic and copies ran while one was open for 10% of the time, Pallas kernels for 0%

profile of v1, /device:TPU:1, one launch (start us, length us, event | category | flops | bytes accessed | tf_op | source)
XLA Modules:
  0.0 239.6 jit_solution(13214018051741657792)
XLA Ops:
  6.5 0.0 copy-start
  6.5 0.0 all-gather.3.cloned.1.call-start
  6.5 1.3 dynamic_slice.21
  9.8 1.2 dynamic_slice.22
  12.4 1.4 fusion.29
  13.7 0.0 copy-start.2
  13.8 0.0 copy-done
  13.8 1.7 fusion.37
  16.2 0.7 constant_dynamic-slice_fusion.2
  18.7 0.3 fusion.46
  19.1 0.6 pad_maximum_fusion.1
  19.7 0.0 all-gather.3.cloned.1.call-update
  19.8 0.7 gather_fusion
  20.5 0.1 copy.32
  20.6 0.1 reshape.420
  20.7 1.1 constant_dynamic-slice_fusion
  21.8 0.0 copy-start.3
  21.8 0.0 copy-start.12
  21.8 1.6 gather_fusion.1
  23.4 8.6 %all-to-all-start = ((bf16[16,2,64,256]{3,2,1,0:T(8,128)(2,1)}), bf16[16,2,64,256]{3,2,1,0:T(8,128)(2,1)}, u32[]{:S(2)}, u32[]{:S(2)}) async-start(bf16[16,2,64,256]{3,2,1,0:T(8,128)(2,1)} %bitcast.8), calls=%async_computation | async-start | bytes 2097152 | tf_op jit(solution)/shard_map/all_to_all | solution.py:73
  32.0 0.0 all-gather.5.cloned.1.call-start
  32.1 1.2 multiply_cosine_fusion
  33.3 0.2 dynamic-slice_reduce_fusion
  33.5 4.4 %fusion.39 = f32[256,1536]{0,1:T(8,128)S(1)} fusion(bf16[1536,1536]{1,0:T(8,128)(2,1)} %param.16, bf16[256,1536]{1,0:T(8,128)(2,1)S(1)} %copy-done.3, f32[1536]{0:T(1024)S(1)} %copy-done.12, f32[256]{0:T(256)S(1)} %add_rsqrt_fusion.1), kind=kOutput, calls=%fused_computation.55 | convolution fusion | flops 1209532416 | bytes 7085056 | tf_op jit(solution)/shard_map/dot_general | solution.py:79
  37.9 0.0 copy-start.5
  37.9 1.0 fusion.64
  38.9 0.0 copy-done.5
  38.9 0.1 copy.36
  39.1 1.6 copy.40
  40.7 1.6 copy.41
  42.3 0.7 fusion.49
  43.0 3.6 %multiply_subtract_fusion = (f32[256,12,64]{2,0,1:T(8,128)}, f32[256,12,64]{2,0,1:T(8,128)}) fusion(f32[256,12,64]{2,0,1:T(8,128)} %copy.41, f32[256,12,64]{2,0,1:T(8,128)S(1)} %copy.40, f32[256,64]{1,0:T(8,128)} %get-tuple-element.17, f32[256,64]{1,0:T(8,128)S(1)} %get-tuple-element.16), kind=kLoop, calls=%fused_computation.49 | loop fusion | flops 1179648 | bytes 3276800 | tf_op jit(solution)/shard_map/sub | solution.py:25
  46.6 1.1 fusion.35
  47.7 0.0 all-to-all-done
  47.7 1.8 gather_fusion.2
  49.5 0.1 copy.33
  49.6 16.5 %all_gather.9 = bf16[2,512,256]{2,0,1:T(2,128)(2,1)S(1)} all-gather(bf16[2,64,256]{2,0,1:T(2,128)(2,1)S(1)} %copy.33), channel_id=1, replica_groups=mesh['req'=16,'mlp'=8] {'mlp'}, dimensions={1}, use_global_device_ids=true | all-gather | bytes 589824 | tf_op jit(solution)/shard_map/all_gather | solution.py:76
  66.1 0.7 fusion.65
  66.8 0.7 copy.42
  67.5 0.7 copy.43
  68.2 0.0 all-gather.3.cloned.1.call-done
  68.2 2.6 %pad_maximum_fusion = bf16[3584,256]{0,1:T(8,128)(2,1)} fusion(bf16[2048,256]{0,1:T(8,128)(2,1)} %all-gather.3.cloned.1.call-done, bf16[512,256]{0,1:T(8,128)(2,1)S(1)} %bitcast.62, bf16[512,256]{0,1:T(8,128)(2,1)S(1)} %bitcast.61, bf16[512,256]{0,1:T(8,128)(2,1)S(1)} %bitcast.60), kind=kLoop, calls=%fused_computation.38 | loop fusion | flops 7340032 | bytes 3670016 | tf_op jit(solution)/shard_map/concatenate | solution.py:88
  70.8 2.9 %copy.37 = bf16[3584,256]{1,0:T(8,128)(2,1)S(1)} copy(bf16[3584,256]{0,1:T(8,128)(2,1)} %pad_maximum_fusion) | data formatting | bytes 3670016 | tf_op jit(solution)/shard_map/concatenate | solution.py:88
  73.7 4.1 %gather_fusion.3 = bf16[1280,256]{1,0:T(8,128)(2,1)S(1)} fusion(bf16[3584,256]{1,0:T(8,128)(2,1)S(1)} %copy.37, s32[2048]{0:T(1024)S(1)} %pad_clamp_fusion), kind=kCustom, calls=%fused_computation.3 | custom fusion | bytes 1315840 | tf_op jit(solution)/shard_map/jit(_take)/gather | solution.py:105
  77.8 0.0 copy-start.4
  77.8 11.6 %fusion.66 = (f32[256,12]{0,1:T(8,128)S(1)}, bf16[256,12,1280]{2,0,1:T(8,128)(2,1)}) fusion(pred[256,1280]{1,0:T(8,128)(4,1)} %fusion.35, bf16[1280,256]{1,0:T(8,128)(2,1)S(1)} %gather_fusion.3, f32[256,12,64]{2,0,1:T(8,128)} %get-tuple-element.6, f32[256,12,64]{2,0,1:T(8,128)} %get-tuple-element.5), kind=kOutput, calls=%fused_computation.116 | convolution fusion | flops 2035287296 | bytes 15478784 | tf_op jit(solution)/shard_map/sub | solution.py:110
  89.4 5.9 %divide_convert_fusion = bf16[256,12,128]{0,2,1:T(8,128)(2,1)S(1)} fusion(bf16[256,12,1280]{2,0,1:T(8,128)(2,1)} %get-tuple-element.19, f32[256,12]{0,1:T(8,128)S(1)} %get-tuple-element.18, bf16[1280,256]{1,0:T(8,128)(2,1)} %copy-done.4), kind=kOutput, calls=%fused_computation.47 | convolution fusion | flops 1007419392 | bytes 8990720 | tf_op jit(solution)/shard_map/thk,kd->thd/dot_general | solution.py:112
  95.3 0.0 copy-start.9
  95.3 3.8 %multiply_reduce_fusion = (f32[256]{0:T(256)S(1)}, f32[256,1536]{1,0:T(8,128)S(1)}) fusion(bf16[256,1536]{0,1:T(8,128)(2,1)S(1)} %bitcast.58, bf16[1536,1536]{1,0:T(8,128)(2,1)} %param.18, bf16[256,1536]{1,0:T(8,128)(2,1)S(1)} %copy-done.3), kind=kOutput, calls=%fused_computation.46 | convolution fusion | flops 1210318592 | bytes 7865344 | tf_op jit(solution)/shard_map/dot_general | solution.py:119
  99.1 0.0 copy-start.6
  99.2 0.0 copy-start.7
  99.2 0.0 copy-start.8
  99.2 1.1 multiply_convert_fusion
  100.3 0.0 all-gather.5.cloned.1.call-update
  100.3 0.0 reduce-scatter.2.cloned.1.call-start
  100.4 0.1 concatenate.47
  100.5 0.5 stack.40
  101.1 68.8 %all_to_all.10 = bf16[16,96,1728]{2,1,0:T(8,128)(2,1)} all-to-all(bf16[16,96,1728]{2,1,0:T(8,128)(2,1)S(1)} %stack.40), channel_id=1, replica_groups=mesh['req'=16,'mlp'=8] {'req'}, dimensions={0} | all-to-all | bytes 10616832 | tf_op jit(solution)/shard_map/all_to_all | solution.py:59
  169.9 11.1 %fusion.17 = f32[2048,1152]{0,1:T(8,128)S(1)} fusion(bf16[2048,1536]{1,0:T(8,128)(2,1)} %all-gather.5.cloned.1.call-done, bf16[1536,1728]{1,0:T(8,128)(2,1)} %bitcast.56), kind=kOutput, calls=%fused_computation.23 | convolution fusion | flops 7247757312 | bytes 19267584 | tf_op jit(solution)/shard_map/dot_general | solution.py:123
  181.0 9.6 %convolution_convert_fusion = bf16[2048,1536]{1,0:T(8,128)(2,1)} fusion(f32[2048,1152]{0,1:T(8,128)S(1)} %fusion.17, bf16[1536,1728]{1,0:T(8,128)(2,1)} %bitcast.57), kind=kOutput, calls=%fused_computation.12 | convolution fusion | flops 3638820864 | bytes 17694720 | tf_op jit(solution)/shard_map/dot_general | solution.py:128
  190.6 0.0 reduce-scatter.2.cloned.1.call-update
  190.6 0.0 copy-start.1
  190.6 40.2 %reduce-scatter.2.cloned.1.call-done = bf16[256,1536]{1,0:T(8,128)(2,1)} async-done(((bf16[2048,1536]{1,0:T(8,128)(2,1)}), bf16[256,1536]{1,0:T(8,128)(2,1)}) %reduce-scatter.2.cloned.1.call-update) | async-done | bytes 786448 | tf_op jit(solution)/shard_map/reduce_scatter | solution.py:127
  230.8 2.2 add_convert_fusion
  (29 shorter events, 0.2 us)
Async XLA Ops:
  6.5 7.2 %copy-start = (bf16[1536,256]{1,0:T(8,128)(2,1)S(1)}, bf16[1536,256]{1,0:T(8,128)(2,1)}, u32[]{:S(2)}) copy-start(bf16[1536,256]{1,0:T(8,128)(2,1)} %param.17) | copy-start | bytes 2359300
  6.5 9.6 %copy-start.11 = (s32[3,128]{1,0:T(4,128)S(1)}, s32[3,128]{1,0:T(4,128)}, u32[]{:S(2)}) copy-start(s32[3,128]{1,0:T(4,128)} %param.27) | copy-start | bytes 4612
  6.5 61.7 %all-gather.3.cloned.1.call-start = ((), (), s32[]{:S(2)}) async-start(), calls=%async_computation.3 | async-start | bytes 1179648 | tf_op jit(solution)/shard_map/all_gather | solution.py:87
  13.7 6.0 %copy-start.10 = (s32[16]{0:T(128)S(1)}, s32[16]{0:T(128)}, u32[]{:S(2)}) copy-start(s32[16]{0:T(128)} %param.25) | copy-start | bytes 196
  13.7 6.1 %copy-start.2 = (s32[128]{0:T(128)S(1)}, s32[128]{0:T(128)}, u32[]{:S(2)}) copy-start(s32[128]{0:T(128)} %param.26) | copy-start | bytes 1540
  21.8 11.8 %copy-start.3 = (bf16[256,1536]{1,0:T(8,128)(2,1)S(1)}, bf16[256,1536]{1,0:T(8,128)(2,1)}, u32[]{:S(2)}) copy-start(bf16[256,1536]{1,0:T(8,128)(2,1)} %param.14) | copy-start | bytes 2359300
  21.8 11.8 %copy-start.12 = (f32[1536]{0:T(1024)S(1)}, f32[1536]{0:T(1024)}, u32[]{:S(2)}) copy-start(f32[1536]{0:T(1024)} %param.15) | copy-start | bytes 18436
  23.4 24.3 %all-to-all-start = ((bf16[16,2,64,256]{3,2,1,0:T(8,128)(2,1)}), bf16[16,2,64,256]{3,2,1,0:T(8,128)(2,1)}, u32[]{:S(2)}, u32[]{:S(2)}) async-start(bf16[16,2,64,256]{3,2,1,0:T(8,128)(2,1)} %bitcast.8), calls=%async_computation | async-start | bytes 2097152 | tf_op jit(solution)/shard_map/all_to_all | solution.py:73
  32.0 137.8 %all-gather.5.cloned.1.call-start = ((), (), s32[]{:S(2)}) async-start(), calls=%async_computation.4 | async-start | bytes 7077888 | tf_op jit(solution)/shard_map/all_gather | solution.py:122
  37.9 1.1 copy-start.5
  77.8 11.6 %copy-start.4 = (bf16[1280,256]{1,0:T(8,128)(2,1)}, bf16[1280,256]{1,0:T(8,128)(2,1)S(1)}, u32[]{:S(2)}) copy-start(bf16[1280,256]{1,0:T(8,128)(2,1)S(1)} %gather_fusion.3) | copy-start | bytes 1966084
  95.3 3.9 %copy-start.9 = (f32[1536]{0:T(1024)S(1)}, f32[1536]{0:T(1024)}, u32[]{:S(2)}) copy-start(f32[1536]{0:T(1024)} %param.19) | copy-start | bytes 18436
  99.1 1.2 copy-start.6
  99.2 1.2 copy-start.7
  99.2 1.2 copy-start.8
  100.3 130.5 %reduce-scatter.2.cloned.1.call-start = ((), (), s32[]{:S(2)}) async-start(), calls=%async_computation.5 | async-start | bytes 7077888 | tf_op jit(solution)/shard_map/reduce_scatter | solution.py:127
  190.6 42.4 %copy-start.1 = (bf16[1536,256]{1,0:T(8,128)(2,1)S(1)}, bf16[1536,256]{1,0:T(8,128)(2,1)}, u32[]{:S(2)}) copy-start(bf16[1536,256]{1,0:T(8,128)(2,1)} %param.17) | copy-start | bytes 2359300
Sparse Core Ops, SparseCore 0:
  19.9 26.9 all-gather.2
  100.4 39.6 all-gather.4
  190.7 40.0 reduce-scatter.1
